TPU v7x, 256 devices: a whole 4x4x8 slice. The times are simulated.
256 devices in a mesh: mem: 32 (over z, x), pipe: 4 (over y), dp: 2 (over core).
Axes of the slice: x: 4, y: 4, z: 8, core: 2. Of those that a mesh axis runs over, the one named last changes fastest.
Arguments:
- values: bfloat16 [32768, 4096], P(('dp', 'mem'), 'pipe'), parts along dimension 0, may hold values from -6 to 6
- cotangent: bfloat16 [8192, 4096], P(('dp', 'mem'), 'pipe'), parts along dimension 0, may hold values from -6 to 6
- scores: float32 [8192, 4, 32], P(('dp', 'mem')), parts along dimension 0, may hold values from -8 to 410, as said below
- row_lists: int32 [64, 32, 128], P(('dp', 'mem')), parts along dimension 0, may hold values from -1 to 511, as said below
- sel_slot: int32 [8192, 4, 32], P(('dp', 'mem')), parts along dimension 0, may hold values from 0 to 4095, as said below
Outputs:
- mem_out: bfloat16 [8192, 4096], P(('dp', 'mem'), 'pipe'), parts along dimension 0
- grad_values: bfloat16 [32768, 4096], P(('dp', 'mem'), 'pipe'), parts along dimension 0
- grad_scores: float32 [8192, 4, 32], P(('dp', 'mem')), parts along dimension 0
There are 2 independent parts, one for each index of `dp`. A program takes and returns all parts, laid end to end along the dimension named above; each array names one. Nothing has to cross between parts.
Inputs may be any that keep to these rules, and one draw needn't show every extreme that they name: `row_lists`: each entry is a row of the owner's shard, or -1 for an empty slot; the rows of one block are distinct and its empty slots come last; in every draw some owner receives full blocks of 128 rows from every device. `sel_slot`: each entry names a slot of the request blocks of the token's own mem index, and that slot holds a row; the 32 entries of one token and head are distinct. `scores`: scores are finite.
All inputs are finite; a program needn't handle non-finite values.
Results may differ from a plain program's by a relative error of at most 0.013.
Values may be sent and summed in bfloat16 or wider, within the bound.
No kernel may reach another device: no remote copies, remote signals or barrier semaphores. Data moves between devices by JAX's collectives and lax.ppermute only.
A program may use at most 128 MiB of HBM per device.

v0:
```python
import jax
import jax.numpy as jnp
from jax import lax
from jax.sharding import PartitionSpec as P


def shards(values, cotangent, scores, row_lists, sel_slot):
    owners = lax.axis_size("mem")
    tokens_here = cotangent.shape[0]
    cap_slots = row_lists.shape[2]
    slot_count = owners * cap_slots
    width = values.shape[1]
    table_rows = values.shape[0]
    highest = lax.Precision.HIGHEST
    weights = jax.nn.softmax(scores, axis=-1)
    chosen = sel_slot.reshape(tokens_here, -1)
    owner_of = chosen // cap_slots
    place_of = chosen % cap_slots
    owner_hot = (owner_of[..., None] == jnp.arange(owners, dtype=jnp.int32)[None, None, :]).astype(
        jnp.float32
    )
    place_hot = (
        place_of[..., None] == jnp.arange(cap_slots, dtype=jnp.int32)[None, None, :]
    ).astype(jnp.float32)
    weighted_owner = owner_hot * weights.reshape(tokens_here, -1)[..., None]
    combined = jnp.einsum(
        "tpo,tpc->toc",
        weighted_owner,
        place_hot,
        precision=highest,
        preferred_element_type=jnp.float32,
    )
    combined = combined.reshape(tokens_here, slot_count).astype(jnp.bfloat16)
    asked = lax.all_to_all(row_lists[0], "mem", split_axis=0, concat_axis=0, tiled=True)
    present = asked >= 0
    looked = jnp.take(values, jnp.maximum(asked, 0), axis=0)
    looked = jnp.where(present[..., None], looked, jnp.zeros_like(looked))
    replied = lax.all_to_all(looked, "mem", split_axis=0, concat_axis=0, tiled=True)
    gathered_rows = replied.reshape(slot_count, width)
    mem_out = jnp.dot(combined, gathered_rows, preferred_element_type=jnp.float32).astype(
        jnp.bfloat16
    )
    products = lax.dot_general(
        cotangent, gathered_rows, (((1,), (1,)), ((), ())), preferred_element_type=jnp.float32
    )
    products = products.reshape(tokens_here, owners, cap_slots)
    picked = jnp.einsum(
        "tpc,toc->tpo", place_hot, products, precision=highest, preferred_element_type=jnp.float32
    )
    partial_dots = jnp.sum(picked * owner_hot, axis=-1).reshape(weights.shape)
    full_dots = lax.psum(partial_dots.astype(jnp.bfloat16), "pipe").astype(jnp.float32)
    grad_scores = weights * (full_dots - jnp.sum(weights * full_dots, axis=-1, keepdims=True))
    sums_here = lax.dot_general(
        combined, cotangent, (((0,), (0,)), ((), ())), preferred_element_type=jnp.float32
    )
    received = lax.all_to_all(
        sums_here.reshape(owners, cap_slots, width).astype(jnp.bfloat16),
        "mem",
        split_axis=0,
        concat_axis=0,
        tiled=True,
    ).astype(jnp.float32)
    received = received.reshape(-1, width)
    upper_part = received.astype(jnp.bfloat16)
    lower_part = (received - upper_part.astype(jnp.float32)).astype(jnp.bfloat16)
    row_hot = (
        asked.reshape(-1)[:, None] == jnp.arange(table_rows, dtype=jnp.int32)[None, :]
    ).astype(jnp.bfloat16)
    contract = (((0,), (0,)), ((), ()))
    grad_full = lax.dot_general(row_hot, upper_part, contract, preferred_element_type=jnp.float32)
    grad_full = grad_full + lax.dot_general(
        row_hot, lower_part, contract, preferred_element_type=jnp.float32
    )
    grad_values = grad_full.astype(jnp.bfloat16)
    return (mem_out, grad_values, grad_scores)


def solution(mesh):
    placed = (
        P(("dp", "mem"), "pipe"),
        P(("dp", "mem"), "pipe"),
        P(("dp", "mem"), None, None),
        P(("dp", "mem"), None, None),
        P(("dp", "mem"), None, None),
    )
    return jax.shard_map(
        shards,
        mesh=mesh,
        in_specs=placed,
        out_specs=(
            P(("dp", "mem"), "pipe"),
            P(("dp", "mem"), "pipe"),
            P(("dp", "mem"), None, None),
        ),
        check_vma=False,
    )
```

profile of v0, /device:TPU:6, one launch (start us, length us, event | category | flops | bytes accessed | tf_op | source)
XLA Modules:
  0.0 464.0 jit_solution(3009705925394027708)
XLA Ops:
  0.6 0.0 copy-start
  0.6 0.0 copy-start.2
  0.7 11.7 %all-to-all-start = ((s32[32,1,128]{2,1,0:T(1,128)}), s32[32,1,128]{2,1,0:T(1,128)S(1)}, u32[]{:S(2)}, u32[]{:S(2)}) async-start(s32[32,1,128]{2,1,0:T(1,128)} %bitcast.53), calls=%async_computation | async-start | bytes 32768 | tf_op jit(solution)/shard_map/all_to_all | solution.py:34
  12.4 1.0 fusion.17
  13.3 0.1 copy.29
  13.4 0.9 copy.25
  14.4 0.1 add_select_fusion.1
  14.4 0.0 copy-start.3
  14.4 5.9 %fusion.12 = bf16[128,32,128]{2,1,0:T(8,128)(2,1)S(1)} fusion(s32[128,128]{1,0:T(8,128)S(1)} %get-tuple-element.4, f32[128,128]{1,0:T(8,128)S(1)} %copy.29, s32[128,128]{1,0:T(8,128)S(1)} %get-tuple-element.3), kind=kOutput, calls=%fused_computation.21 | convolution fusion | flops 808976384 | bytes 1245184 | tf_op jit(solution)/shard_map/tpo,tpc->toc/dot_general | solution.py:26
  20.3 0.0 copy-start.1
  20.3 1.0 copy-done.1
  21.3 0.5 copy.40
  21.8 0.0 copy-done.3
  21.8 0.7 copy.33
  22.4 0.0 copy-done.2
  22.4 5.6 %convolution_convert_fusion = bf16[32,128,1024]{2,1,0:T(8,128)(2,1)} fusion(bf16[32,128,128]{2,1,0:T(8,128)(2,1)S(1)} %bitcast.44, bf16[128,1024]{1,0:T(8,128)(2,1)S(1)} %copy-done.2), kind=kOutput, calls=%fused_computation.12 | convolution fusion | flops 1077936128 | bytes 9699328 | tf_op jit(solution)/shard_map/dot_general | solution.py:53
  28.0 0.0 all-to-all-done
  28.0 9.8 %all-to-all-start.2 = ((bf16[32,128,1024]{2,1,0:T(8,128)(2,1)}), bf16[32,128,1024]{2,1,0:T(8,128)(2,1)}, u32[]{:S(2)}, u32[]{:S(2)}) async-start(bf16[32,128,1024]{2,1,0:T(8,128)(2,1)} %convolution_convert_fusion), calls=%async_computation.2 | async-start | bytes 16777216 | tf_op jit(solution)/shard_map/all_to_all | solution.py:56
  37.9 0.0 copy-done
  37.9 18.3 %gather_fusion = bf16[4096,1024]{1,0:T(8,128)(2,1)} fusion(bf16[512,1024]{1,0:T(8,128)(2,1)S(1)} %copy-done, s32[4096]{0:T(1024)S(1)} %bitcast_clamp_fusion), kind=kCustom, calls=%fused_computation | custom fusion | bytes 16793600 | tf_op jit(solution)/shard_map/jit(_take)/gather | solution.py:36
  56.1 7.5 %select_select_fusion = bf16[32,128,1024]{2,1,0:T(8,128)(2,1)} fusion(bf16[32,128,1024]{2,1,0:T(8,128)(2,1)} %bitcast.41, pred[32,128]{1,0:T(8,128)(4,1)S(1)} %get-tuple-element.6, pred[32,128]{1,0:T(8,128)(4,1)S(1)} %get-tuple-element.5), kind=kLoop, calls=%fused_computation.8 | loop fusion | flops 8388608 | bytes 16785408 | tf_op jit(solution)/shard_map/jit(_where)/select_n | solution.py:37
  63.6 164.4 %all-to-all-done.2 = bf16[32,128,1024]{2,1,0:T(8,128)(2,1)} async-done(((bf16[32,128,1024]{2,1,0:T(8,128)(2,1)}), bf16[32,128,1024]{2,1,0:T(8,128)(2,1)}, u32[]{:S(2)}, u32[]{:S(2)}) %all-to-all-start.2) | async-done | bytes 8388640 | tf_op jit(solution)/shard_map/all_to_all | solution.py:56
  228.0 7.7 %all-to-all-start.1 = ((bf16[32,128,1024]{2,1,0:T(8,128)(2,1)}), bf16[32,128,1024]{2,1,0:T(8,128)(2,1)}, u32[]{:S(2)}, u32[]{:S(2)}) async-start(bf16[32,128,1024]{2,1,0:T(8,128)(2,1)} %select_select_fusion), calls=%async_computation.1 | async-start | bytes 16777216 | tf_op jit(solution)/shard_map/all_to_all | solution.py:38
  235.7 8.0 %fusion.4 = f32[512,1024]{1,0:T(8,128)S(1)} fusion(bf16[4096,1024]{1,0:T(8,128)(2,1)} %bitcast.14, s32[4096]{0:T(1024)S(1)} %bitcast.49), kind=kOutput, calls=%fused_computation.7 | convolution fusion | flops 4297064448 | bytes 10502144 | tf_op jit(solution)/shard_map/dot_general | solution.py:70
  243.7 9.0 %add_convert_fusion = bf16[512,1024]{1,0:T(8,128)(2,1)} fusion(f32[512,1024]{1,0:T(8,128)S(1)} %fusion.4, bf16[4096,1024]{1,0:T(8,128)(2,1)} %bitcast.14, s32[4096]{0:T(1024)S(1)} %bitcast.50), kind=kOutput, calls=%fused_computation.18 | convolution fusion | flops 4310695936 | bytes 11550720 | tf_op jit(solution)/shard_map/dot_general | solution.py:71
  252.7 170.7 %all-to-all-done.1 = bf16[32,128,1024]{2,1,0:T(8,128)(2,1)} async-done(((bf16[32,128,1024]{2,1,0:T(8,128)(2,1)}), bf16[32,128,1024]{2,1,0:T(8,128)(2,1)}, u32[]{:S(2)}, u32[]{:S(2)}) %all-to-all-start.1) | async-done | bytes 8388640 | tf_op jit(solution)/shard_map/all_to_all | solution.py:38
  423.3 5.7 %fusion.31 = f32[4096,128]{1,0:T(8,128)S(1)} fusion(bf16[4096,1024]{1,0:T(8,128)(2,1)} %bitcast.15, bf16[128,1024]{1,0:T(8,128)(2,1)S(1)} %copy-done.2), kind=kOutput, calls=%fused_computation.50 | convolution fusion | flops 1073741824 | bytes 10747904 | tf_op jit(solution)/shard_map/dot_general | solution.py:43
  429.1 2.2 copy.34
  431.3 8.4 %select_reduce_fusion = bf16[128,128]{1,0:T(8,128)(2,1)S(1)} fusion(f32[128,32,128]{2,1,0:T(8,128)} %copy.34, s32[128,128]{1,0:T(8,128)} %copy-done.3, s32[128,128]{1,0:T(8,128)S(1)} %get-tuple-element.3), kind=kOutput, calls=%fused_computation.17 | convolution fusion | flops 808960000 | bytes 2260992 | tf_op jit(solution)/shard_map/tpc,toc->tpo/dot_general | solution.py:47
  439.7 0.1 copy.35
  439.9 17.5 %psum.7 = bf16[128,4,32]{0,2,1:T(8,128)(2,1)S(1)} all-reduce(bf16[128,4,32]{0,2,1:T(8,128)(2,1)S(1)} %bitcast.51), channel_id=1, replica_groups=mesh['mem'=32,'pipe'=4,'dp'=2] {'pipe'}, use_global_device_ids=true, to_apply=%region_3.4 | all-reduce | flops 16384 | bytes 65536 | tf_op jit(solution)/shard_map/psum | solution.py:51
  457.4 0.7 fusion.20
  458.0 5.9 %fusion.15 = bf16[128,1024]{1,0:T(8,128)(2,1)} fusion(bf16[32,128,1024]{2,1,0:T(8,128)(2,1)} %all-to-all-done.1, bf16[128,32,128]{2,1,0:T(8,128)(2,1)} %copy-done.1), kind=kOutput, calls=%fused_computation.23 | convolution fusion | flops 1073872896 | bytes 9699328 | tf_op jit(solution)/shard_map/dot_general | solution.py:40
  (2 shorter events, 0.0 us)
Async XLA Ops:
  0.6 37.2 %copy-start = (bf16[512,1024]{1,0:T(8,128)(2,1)S(1)}, bf16[512,1024]{1,0:T(8,128)(2,1)}, u32[]{:S(2)}) copy-start(bf16[512,1024]{1,0:T(8,128)(2,1)} %param.5) | copy-start | bytes 3145732
  0.6 21.8 %copy-start.2 = (bf16[128,1024]{1,0:T(8,128)(2,1)S(1)}, bf16[128,1024]{1,0:T(8,128)(2,1)}, u32[]{:S(2)}) copy-start(bf16[128,1024]{1,0:T(8,128)(2,1)} %param.6) | copy-start | bytes 786436
  0.7 27.4 %all-to-all-start = ((s32[32,1,128]{2,1,0:T(1,128)}), s32[32,1,128]{2,1,0:T(1,128)S(1)}, u32[]{:S(2)}, u32[]{:S(2)}) async-start(s32[32,1,128]{2,1,0:T(1,128)} %bitcast.53), calls=%async_computation | async-start | bytes 32768 | tf_op jit(solution)/shard_map/all_to_all | solution.py:34
  14.4 7.3 %copy-start.3 = (s32[128,128]{1,0:T(8,128)}, s32[128,128]{1,0:T(8,128)S(1)}, u32[]{:S(2)}) copy-start(s32[128,128]{1,0:T(8,128)S(1)} %get-tuple-element.4) | copy-start | bytes 196612
  20.3 1.0 copy-start.1
  28.0 200.0 %all-to-all-start.2 = ((bf16[32,128,1024]{2,1,0:T(8,128)(2,1)}), bf16[32,128,1024]{2,1,0:T(8,128)(2,1)}, u32[]{:S(2)}, u32[]{:S(2)}) async-start(bf16[32,128,1024]{2,1,0:T(8,128)(2,1)} %convolution_convert_fusion), calls=%async_computation.2 | async-start | bytes 16777216 | tf_op jit(solution)/shard_map/all_to_all | solution.py:56
  228.0 195.3 %all-to-all-start.1 = ((bf16[32,128,1024]{2,1,0:T(8,128)(2,1)}), bf16[32,128,1024]{2,1,0:T(8,128)(2,1)}, u32[]{:S(2)}, u32[]{:S(2)}) async-start(bf16[32,128,1024]{2,1,0:T(8,128)(2,1)} %select_select_fusion), calls=%async_computation.1 | async-start | bytes 16777216 | tf_op jit(solution)/shard_map/all_to_all | solution.py:38
where the time goes:
time: 465 us; the launch traced here: 464 us
  waiting for transfers between devices  335 us (72%)
  matrix products  48.5 us (10%)
  starting transfers between devices  29.2 us (6%)
  local copies, waits for them, and re-layouts  23.7 us (5%)
  blocking collectives  17.5 us (4%)
  other arithmetic  9.16 us (2%)
    all_to_all x1, waiting for transfers between devices, shards(): lax.all_to_all(looked, 'mem', split_axis=0, concat_axis=0, tiled=True)  171 us
    all_to_all x1, waiting for transfers between devices, shards(): lax.all_to_all(sums_here.reshape(owners, cap_slots, width).astype(jnp.bfl...  164 us
    gather x1, local copies, waits for them, and re-layouts, shards(): looked = jnp.take(values, jnp.maximum(asked, 0), axis=0)  18.3 us
    psum x1, blocking collectives, shards(): lax.psum(partial_dots.astype(jnp.bfloat16), 'pipe').astype(jnp.float32)  17.5 us
    all_to_all x1, starting transfers between devices, shards(): lax.all_to_all(row_lists[0], 'mem', split_axis=0, concat_axis=0, tiled=True)  11.7 us
    all_to_all x1, starting transfers between devices, shards(): lax.all_to_all(sums_here.reshape(owners, cap_slots, width).astype(jnp.bfl...  9.83 us
  transfers between devices with their start and end apart: 3, of which 2 were waited for; matrix products, arithmetic and copies ran while one was open for 12% of the time, Pallas kernels for 0%

commit v1 on v0

--- a/solution.py
+++ b/solution.py
@@ -4,7 +4,7 @@
 from jax.sharding import PartitionSpec as P
 
 
-def shards(values, cotangent, scores, row_lists, sel_slot):
+def body(values, cotangent, scores, row_lists, sel_slot):
     owners = lax.axis_size("mem")
     tokens_here = cotangent.shape[0]
     cap_slots = row_lists.shape[2]
@@ -31,11 +31,20 @@
         preferred_element_type=jnp.float32,
     )
     combined = combined.reshape(tokens_here, slot_count).astype(jnp.bfloat16)
+    sums_here = lax.dot_general(
+        combined, cotangent, (((0,), (0,)), ((), ())), preferred_element_type=jnp.float32
+    ).astype(jnp.bfloat16)
+    received = lax.all_to_all(
+        sums_here.reshape(owners, cap_slots, width), "mem", 0, 0, tiled=True
+    ).reshape(-1, width)
     asked = lax.all_to_all(row_lists[0], "mem", split_axis=0, concat_axis=0, tiled=True)
-    present = asked >= 0
-    looked = jnp.take(values, jnp.maximum(asked, 0), axis=0)
-    looked = jnp.where(present[..., None], looked, jnp.zeros_like(looked))
-    replied = lax.all_to_all(looked, "mem", split_axis=0, concat_axis=0, tiled=True)
+    row_hot = (
+        asked.reshape(-1)[:, None] == jnp.arange(table_rows, dtype=jnp.int32)[None, :]
+    ).astype(jnp.bfloat16)
+    looked = jnp.dot(row_hot, values, preferred_element_type=jnp.float32).astype(jnp.bfloat16)
+    replied = lax.all_to_all(
+        looked.reshape(owners, cap_slots, width), "mem", 0, 0, tiled=True
+    )
     gathered_rows = replied.reshape(slot_count, width)
     mem_out = jnp.dot(combined, gathered_rows, preferred_element_type=jnp.float32).astype(
         jnp.bfloat16
@@ -50,27 +59,8 @@
     partial_dots = jnp.sum(picked * owner_hot, axis=-1).reshape(weights.shape)
     full_dots = lax.psum(partial_dots.astype(jnp.bfloat16), "pipe").astype(jnp.float32)
     grad_scores = weights * (full_dots - jnp.sum(weights * full_dots, axis=-1, keepdims=True))
-    sums_here = lax.dot_general(
-        combined, cotangent, (((0,), (0,)), ((), ())), preferred_element_type=jnp.float32
-    )
-    received = lax.all_to_all(
-        sums_here.reshape(owners, cap_slots, width).astype(jnp.bfloat16),
-        "mem",
-        split_axis=0,
-        concat_axis=0,
-        tiled=True,
-    ).astype(jnp.float32)
-    received = received.reshape(-1, width)
-    upper_part = received.astype(jnp.bfloat16)
-    lower_part = (received - upper_part.astype(jnp.float32)).astype(jnp.bfloat16)
-    row_hot = (
-        asked.reshape(-1)[:, None] == jnp.arange(table_rows, dtype=jnp.int32)[None, :]
-    ).astype(jnp.bfloat16)
     contract = (((0,), (0,)), ((), ()))
-    grad_full = lax.dot_general(row_hot, upper_part, contract, preferred_element_type=jnp.float32)
-    grad_full = grad_full + lax.dot_general(
-        row_hot, lower_part, contract, preferred_element_type=jnp.float32
-    )
+    grad_full = lax.dot_general(row_hot, received, contract, preferred_element_type=jnp.float32)
     grad_values = grad_full.astype(jnp.bfloat16)
     return (mem_out, grad_values, grad_scores)
 
@@ -84,7 +74,7 @@
         P(("dp", "mem"), None, None),
     )
     return jax.shard_map(
-        shards,
+        body,
         mesh=mesh,
         in_specs=placed,
         out_specs=(

time: 465 us -> 463 us (level)
  waiting for transfers between devices: 335 us -> 364 us
  local copies, waits for them, and re-layouts: 23.7 us -> 4.25 us
  other arithmetic: 9.16 us -> 1.67 us
    all_to_all x3, waiting for transfers between devices: 335 us -> 364 us  [the longest x1 183 us: body(): lax.all_to_all(sums_here.reshape(owners, cap_slots, width), 'mem', 0, 0,...]
    gather x1 -> x0, local copies, waits for them, and re-layouts: 18.3 us -> none  [shards(): looked = jnp.take(values, jnp.maximum(asked, 0), axis=0)]
    select_n x2 -> x1, other arithmetic: 7.53 us -> 0.06 us  [body(): owner_of = chosen // cap_slots]
  transfers between devices with their start and end apart: 3 -> 3, of which waited for: 2 -> 2; matrix products, arithmetic and copies ran while one was open for 12% -> 6% of each run, Pallas kernels for 0% -> 0%
where the time goes in v1:
time: 463 us
  waiting for transfers between devices  364 us (79%)
  matrix products  47 us (10%)
  starting transfers between devices  29.3 us (6%)
  blocking collectives  16.1 us (3%)
    all_to_all x1, waiting for transfers between devices, body(): lax.all_to_all(sums_here.reshape(owners, cap_slots, width), 'mem', 0, 0,...  183 us
    all_to_all x1, waiting for transfers between devices, body(): lax.all_to_all(looked.reshape(owners, cap_slots, width), 'mem', 0, 0, til...  181 us
    psum x1, blocking collectives, body(): lax.psum(partial_dots.astype(jnp.bfloat16), 'pipe').astype(jnp.float32)  16.1 us
    all_to_all x1, starting transfers between devices, body(): lax.all_to_all(row_lists[0], 'mem', split_axis=0, concat_axis=0, tiled=True)  11.7 us
    all_to_all x1, starting transfers between devices, body(): lax.all_to_all(sums_here.reshape(owners, cap_slots, width), 'mem', 0, 0,...  9.83 us
  transfers between devices with their start and end apart: 3, of which 2 were waited for; matrix products, arithmetic and copies ran while one was open for 6% of the time, Pallas kernels for 0%

profile of v1, /device:TPU:6, one launch (start us, length us, event | category | flops | bytes accessed | tf_op | source)
XLA Modules:
  0.0 462.6 jit_solution(7690465694453646406)
XLA Ops:
  0.6 0.0 copy-start
  0.6 11.7 %all-to-all-start = ((s32[32,1,128]{2,1,0:T(1,128)}), s32[32,1,128]{2,1,0:T(1,128)S(1)}, u32[]{:S(2)}, u32[]{:S(2)}) async-start(s32[32,1,128]{2,1,0:T(1,128)} %bitcast.35), calls=%async_computation | async-start | bytes 32768 | tf_op jit(solution)/shard_map/all_to_all | solution.py:40
  12.4 0.9 copy.23
  13.3 0.1 add_select_fusion.1
  13.4 0.0 copy-start.4
  13.4 1.0 fusion.19
  14.3 0.1 copy.27
  14.4 0.0 copy-start.3
  14.4 5.9 %fusion.14 = bf16[128,32,128]{2,1,0:T(8,128)(2,1)S(1)} fusion(s32[128,128]{1,0:T(8,128)S(1)} %get-tuple-element.4, f32[128,128]{1,0:T(8,128)S(1)} %copy.27, s32[128,128]{1,0:T(8,128)S(1)} %get-tuple-element.3), kind=kOutput, calls=%fused_computation.19 | convolution fusion | flops 808976384 | bytes 1245184 | tf_op jit(solution)/shard_map/tpo,tpc->toc/dot_general | solution.py:26
  20.3 0.0 copy-done.4
  20.3 0.0 copy-start.1
  20.3 1.1 copy-done.1
  21.4 0.0 copy-done.3
  21.4 5.6 %convolution_convert_fusion = bf16[4096,1024]{1,0:T(8,128)(2,1)} fusion(bf16[128,1024]{1,0:T(8,128)(2,1)S(1)} %copy-done.3, bf16[16,8,32,128]{3,2,1,0:T(8,128)(2,1)S(1)} %bitcast.30), kind=kOutput, calls=%fused_computation.10 | convolution fusion | flops 1077936128 | bytes 9699328 | tf_op jit(solution)/shard_map/dot_general | solution.py:34
  27.0 0.0 all-to-all-done
  27.0 9.8 %all-to-all-start.2 = ((bf16[32,128,1024]{2,1,0:T(8,128)(2,1)}), bf16[32,128,1024]{2,1,0:T(8,128)(2,1)}, u32[]{:S(2)}, u32[]{:S(2)}) async-start(bf16[32,128,1024]{2,1,0:T(8,128)(2,1)} %bitcast.28), calls=%async_computation.2 | async-start | bytes 16777216 | tf_op jit(solution)/shard_map/all_to_all | solution.py:37
  36.9 0.0 copy-done
  36.9 6.8 %fusion.7 = bf16[4096,1024]{1,0:T(8,128)(2,1)} fusion(bf16[512,1024]{1,0:T(8,128)(2,1)S(1)} %copy-done, s32[4096]{0:T(1024)S(1)} %bitcast.36), kind=kOutput, calls=%fused_computation.9 | convolution fusion | flops 4301258752 | bytes 9453568 | tf_op jit(solution)/shard_map/dot_general | solution.py:44
  43.7 183.0 %all-to-all-done.2 = bf16[32,128,1024]{2,1,0:T(8,128)(2,1)} async-done(((bf16[32,128,1024]{2,1,0:T(8,128)(2,1)}), bf16[32,128,1024]{2,1,0:T(8,128)(2,1)}, u32[]{:S(2)}, u32[]{:S(2)}) %all-to-all-start.2) | async-done | bytes 8388640 | tf_op jit(solution)/shard_map/all_to_all | solution.py:37
  226.7 7.8 %all-to-all-start.1 = ((bf16[32,128,1024]{2,1,0:T(8,128)(2,1)}), bf16[32,128,1024]{2,1,0:T(8,128)(2,1)}, u32[]{:S(2)}, u32[]{:S(2)}) async-start(bf16[32,128,1024]{2,1,0:T(8,128)(2,1)} %bitcast.31), calls=%async_computation.1 | async-start | bytes 16777216 | tf_op jit(solution)/shard_map/all_to_all | solution.py:45
  234.5 9.0 %fusion.13 = bf16[512,1024]{1,0:T(8,128)(2,1)} fusion(bf16[4096,1024]{1,0:T(8,128)(2,1)} %bitcast.7, s32[4096]{0:T(1024)S(1)} %bitcast.37), kind=kOutput, calls=%fused_computation.18 | convolution fusion | flops 4297588736 | bytes 9453568 | tf_op jit(solution)/shard_map/dot_general | solution.py:63
  243.4 180.5 %all-to-all-done.1 = bf16[32,128,1024]{2,1,0:T(8,128)(2,1)} async-done(((bf16[32,128,1024]{2,1,0:T(8,128)(2,1)}), bf16[32,128,1024]{2,1,0:T(8,128)(2,1)}, u32[]{:S(2)}, u32[]{:S(2)}) %all-to-all-start.1) | async-done | bytes 8388640 | tf_op jit(solution)/shard_map/all_to_all | solution.py:45
  423.9 5.7 %fusion.34 = f32[4096,128]{1,0:T(8,128)S(1)} fusion(bf16[4096,1024]{1,0:T(8,128)(2,1)} %bitcast.8, bf16[128,1024]{1,0:T(8,128)(2,1)S(1)} %copy-done.3), kind=kOutput, calls=%fused_computation.45 | convolution fusion | flops 1073741824 | bytes 10747904 | tf_op jit(solution)/shard_map/dot_general | solution.py:52
  429.7 0.0 copy-start.5
  429.7 2.0 copy.29
  431.7 0.0 copy-done.5
  431.7 0.0 copy-start.2
  431.7 8.5 %select_reduce_fusion = bf16[128,128]{1,0:T(8,128)(2,1)S(1)} fusion(f32[128,32,128]{2,1,0:T(8,128)} %copy.29, s32[128,128]{1,0:T(8,128)S(1)} %copy-done.5, s32[128,128]{1,0:T(8,128)S(1)} %get-tuple-element.3), kind=kOutput, calls=%fused_computation.15 | convolution fusion | flops 808960000 | bytes 2260992 | tf_op jit(solution)/shard_map/tpc,toc->tpo/dot_general | solution.py:56
  440.2 0.1 copy.30
  440.3 16.1 %psum.7 = bf16[128,4,32]{0,2,1:T(8,128)(2,1)S(1)} all-reduce(bf16[128,4,32]{0,2,1:T(8,128)(2,1)S(1)} %bitcast.33), channel_id=1, replica_groups=mesh['mem'=32,'pipe'=4,'dp'=2] {'pipe'}, use_global_device_ids=true, to_apply=%region_3.4 | all-reduce | flops 16384 | bytes 65536 | tf_op jit(solution)/shard_map/psum | solution.py:60
  456.4 0.7 fusion.22
  457.1 0.0 copy-done.2
  457.1 5.6 %fusion.17 = bf16[128,1024]{1,0:T(8,128)(2,1)} fusion(bf16[32,128,1024]{2,1,0:T(8,128)(2,1)} %all-to-all-done.1, bf16[128,32,128]{2,1,0:T(8,128)(2,1)S(1)} %copy-done.2), kind=kOutput, calls=%fused_computation.21 | convolution fusion | flops 1073872896 | bytes 9699328 | tf_op jit(solution)/shard_map/dot_general | solution.py:49
Async XLA Ops:
  0.6 36.3 %copy-start = (bf16[512,1024]{1,0:T(8,128)(2,1)S(1)}, bf16[512,1024]{1,0:T(8,128)(2,1)}, u32[]{:S(2)}) copy-start(bf16[512,1024]{1,0:T(8,128)(2,1)} %param.5) | copy-start | bytes 3145732
  0.6 26.4 %all-to-all-start = ((s32[32,1,128]{2,1,0:T(1,128)}), s32[32,1,128]{2,1,0:T(1,128)S(1)}, u32[]{:S(2)}, u32[]{:S(2)}) async-start(s32[32,1,128]{2,1,0:T(1,128)} %bitcast.35), calls=%async_computation | async-start | bytes 32768 | tf_op jit(solution)/shard_map/all_to_all | solution.py:40
  13.4 7.0 %copy-start.4 = (s32[128,128]{1,0:T(8,128)}, s32[128,128]{1,0:T(8,128)S(1)}, u32[]{:S(2)}) copy-start(s32[128,128]{1,0:T(8,128)S(1)} %get-tuple-element.4) | copy-start | bytes 196612
  14.4 7.0 %copy-start.3 = (bf16[128,1024]{1,0:T(8,128)(2,1)S(1)}, bf16[128,1024]{1,0:T(8,128)(2,1)}, u32[]{:S(2)}) copy-start(bf16[128,1024]{1,0:T(8,128)(2,1)} %param.6) | copy-start | bytes 786436
  20.3 1.1 copy-start.1
  27.0 199.6 %all-to-all-start.2 = ((bf16[32,128,1024]{2,1,0:T(8,128)(2,1)}), bf16[32,128,1024]{2,1,0:T(8,128)(2,1)}, u32[]{:S(2)}, u32[]{:S(2)}) async-start(bf16[32,128,1024]{2,1,0:T(8,128)(2,1)} %bitcast.28), calls=%async_computation.2 | async-start | bytes 16777216 | tf_op jit(solution)/shard_map/all_to_all | solution.py:37
  226.7 197.3 %all-to-all-start.1 = ((bf16[32,128,1024]{2,1,0:T(8,128)(2,1)}), bf16[32,128,1024]{2,1,0:T(8,128)(2,1)}, u32[]{:S(2)}, u32[]{:S(2)}) async-start(bf16[32,128,1024]{2,1,0:T(8,128)(2,1)} %bitcast.31), calls=%async_computation.1 | async-start | bytes 16777216 | tf_op jit(solution)/shard_map/all_to_all | solution.py:45
  429.7 2.0 copy-start.5
  431.7 25.3 %copy-start.2 = (bf16[128,32,128]{2,1,0:T(8,128)(2,1)S(1)}, bf16[128,32,128]{2,1,0:T(8,128)(2,1)}, u32[]{:S(2)}) copy-start(bf16[128,32,128]{2,1,0:T(8,128)(2,1)} %copy-done.1) | copy-start | bytes 3145732
